TPU v7x, 256 devices: a whole 4x4x8 slice. The times are simulated.
256 devices in a mesh: ctx: 16 (over z_lo, x, core), tp: 16 (over z_hi, y).
Axes of the slice: x: 4, y: 4, z: 8 (z_hi: 4, z_lo: 2; z = z_hi * 2 + z_lo), core: 2. Of those that a mesh axis runs over, the one named last changes fastest.
Arguments:
- tokens: bfloat16 [8192, 8192], P('ctx'), may hold values from -40 to 40
- doc_lengths: int32 [8], replicated, may hold values from 1 to 4096, 8192 in all
- w_query: bfloat16 [8192, 4096], P('ctx', 'tp'), may hold values from -0.0625 to 0.0625
- w_key: bfloat16 [8192, 512], P('ctx', 'tp'), may hold values from -0.0625 to 0.0625
- w_value: bfloat16 [8192, 512], P('ctx', 'tp'), may hold values from -0.0625 to 0.0625
- w_output: bfloat16 [4096, 8192], P('tp', 'ctx'), may hold values from -0.09375 to 0.09375
Outputs:
- layer_out: bfloat16 [8192, 8192], P(('ctx', 'tp'))
Inputs may be any that keep to these rules, and one draw needn't show every extreme that they name: `doc_lengths`: the 8 documents lie in order in the sequence, their lengths sum to 8192 and the longest has exactly 4096 tokens.
All inputs are finite; a program needn't handle non-finite values.
Results may differ from a plain program's by a relative error of at most 0.015.
Values may be sent and summed in bfloat16 or wider, within the bound.
No kernel may reach another device: no remote copies, remote signals or barrier semaphores. Data moves between devices by JAX's collectives and lax.ppermute only.
A program may use at most 64 MiB of HBM per device.

v0:
```python
import jax
import jax.numpy as jnp
from jax import lax
from jax.sharding import PartitionSpec as P

HD = 128
HEADS = 32
KVH = 4
DOC_MOST = 4096
rope_base = 500000.0


def rotate(field, positions):
    half_dim = field.shape[-1] // 2
    inverse_freq = rope_base ** (-2.0 * jnp.arange(half_dim, dtype=jnp.float32) / field.shape[-1])
    angles = positions.astype(jnp.float32)[:, None] * inverse_freq[None, :]
    cosine = jnp.cos(angles)[:, None, :]
    sine_part = jnp.sin(angles)[:, None, :]
    first_half = field[..., :half_dim]
    second_half = field[..., half_dim:]
    return jnp.concatenate(
        [
            first_half * cosine - second_half * sine_part,
            second_half * cosine + first_half * sine_part,
        ],
        axis=-1,
    )


def doc_of(positions, doc_starts):
    return jnp.sum((positions[:, None] >= doc_starts[None, :]).astype(jnp.int32), axis=1)


def on_device(tokens, doc_lengths, w_query, w_key, w_value, w_output):
    tok_rows = tokens.shape[0]
    n_tp = lax.axis_size("tp")
    ctx_index = lax.axis_index("ctx")
    tp_index = lax.axis_index("tp")
    first_row = ctx_index * tok_rows
    positions = first_row + jnp.arange(tok_rows, dtype=jnp.int32)
    doc_starts = jnp.cumsum(doc_lengths) - doc_lengths
    doc_ids = doc_of(positions, doc_starts)
    q_cols = w_query.shape[1]
    k_cols = w_key.shape[1]
    w_kv = jnp.concatenate([w_key, w_value], axis=1)
    n_ctx_all = lax.axis_size("ctx")
    ring = [w_kv]
    for shift in range(1, n_ctx_all):
        ring.append(
            lax.ppermute(w_kv, "ctx", [(i, (i + shift) % n_ctx_all) for i in range(n_ctx_all)])
        )
    ring = jnp.stack(ring)
    sources = (ctx_index - jnp.arange(n_ctx_all, dtype=jnp.int32)) % n_ctx_all
    w_kv_full = jnp.take(ring, sources, axis=0).reshape(n_ctx_all * tok_rows, w_kv.shape[1])
    kv_local = jnp.dot(tokens, w_kv_full, preferred_element_type=jnp.float32).astype(jnp.bfloat16)
    w_q_full = lax.all_gather(w_query, "ctx", axis=0, tiled=True)
    query_sum = jnp.dot(tokens, w_q_full, preferred_element_type=jnp.float32)
    heads_dev = q_cols // HD
    query = rotate(query_sum.reshape(tok_rows, heads_dev, HD), positions).astype(jnp.bfloat16)
    dd = k_cols // KVH
    group = HEADS // KVH
    kv_local = kv_local.reshape(tok_rows, 2, dd, KVH)
    dest_heads = jnp.arange(n_tp, dtype=jnp.int32) * heads_dev // group
    pieces = jnp.take(kv_local, dest_heads, axis=3)
    pieces = jnp.transpose(pieces, (3, 0, 1, 2))
    got = lax.all_to_all(pieces, "tp", 0, 0, tiled=False)
    kv_own = jnp.transpose(got, (1, 2, 0, 3)).reshape(tok_rows, 2, n_tp * dd)
    key_raw = kv_own[:, 0, :]
    value_own = kv_own[:, 1, :]
    key_rot = rotate(key_raw.astype(jnp.float32)[:, None, :], positions)[:, 0, :].astype(
        jnp.bfloat16
    )
    kv_rows_local = jnp.concatenate([key_rot, value_own], axis=1)
    n_ctx = lax.axis_size("ctx")
    back = min(n_ctx - 1, -(-(DOC_MOST - 1) // tok_rows))
    slots = []
    for shift in range(back, 0, -1):
        slots.append(
            lax.ppermute(kv_rows_local, "ctx", [(i, i + shift) for i in range(n_ctx - shift)])
        )
    slots.append(kv_rows_local)
    kv_win = jnp.concatenate(slots, axis=0)
    window = kv_win.shape[0]
    key_start = (ctx_index - back) * tok_rows
    key_win = kv_win[:, :HD]
    value_win = kv_win[:, HD:]
    key_positions = key_start + jnp.arange(window, dtype=jnp.int32)
    key_docs = jnp.where(key_positions >= 0, doc_of(key_positions, doc_starts), -1)
    score_scale = HD ** (-0.5)
    n_split = 2
    part_rows = tok_rows // n_split
    q_parts = jnp.transpose(query, (1, 0, 2)).reshape(heads_dev * n_split, part_rows, HD)
    pos_parts = jnp.tile(positions.reshape(n_split, part_rows), (heads_dev, 1))
    doc_parts = jnp.tile(doc_ids.reshape(n_split, part_rows), (heads_dev, 1))

    def one_part(args):
        q_part, pos_part, doc_part = args
        allowed = (key_positions[None, :] <= pos_part[:, None]) & (
            key_docs[None, :] == doc_part[:, None]
        )
        scores = jnp.dot(q_part, key_win.T, preferred_element_type=jnp.float32) * score_scale
        masked = jnp.where(allowed, scores, -jnp.inf)
        row_max = jnp.max(masked, axis=-1, keepdims=True)
        expo = jnp.where(allowed, jnp.exp(masked - row_max), 0.0)
        row_total = jnp.sum(expo, axis=-1, keepdims=True)
        mixed = jnp.dot(expo.astype(jnp.bfloat16), value_win, preferred_element_type=jnp.float32)
        return (mixed / row_total).astype(jnp.bfloat16)

    attended = lax.map(one_part, (q_parts, pos_parts, doc_parts))
    attended = attended.reshape(heads_dev, tok_rows, HD)
    attended = jnp.transpose(attended, (1, 0, 2)).reshape(tok_rows, heads_dev * HD)
    w_moved = lax.ppermute(
        w_output,
        ("ctx", "tp"),
        [(c * n_tp + t, t * n_tp + c) for c in range(n_ctx_all) for t in range(n_tp)],
    )
    w_chunk = lax.all_gather(w_moved, "ctx", axis=0, tiled=True)
    attended_all = lax.all_gather(attended, "tp", axis=1, tiled=True)
    out_chunk = jnp.dot(attended_all, w_chunk, preferred_element_type=jnp.float32).astype(
        jnp.bfloat16
    )
    chunk = out_chunk.shape[1]
    out_rows = tok_rows // n_tp
    sent = out_chunk.reshape(n_tp, out_rows, chunk)
    got_rows = lax.all_to_all(sent, "tp", 0, 0, tiled=False)
    return jnp.transpose(got_rows, (1, 0, 2)).reshape(out_rows, n_tp * chunk)


def solution(mesh):
    placed = (P("ctx", None), P(), P("ctx", "tp"), P("ctx", "tp"), P("ctx", "tp"), P("tp", "ctx"))
    return jax.shard_map(
        on_device, mesh=mesh, in_specs=placed, out_specs=P(("ctx", "tp"), None), check_vma=False
    )
```

profile of v0, /device:TPU:6, one launch (start us, length us, event | category | flops | bytes accessed | tf_op | source)
XLA Modules:
  0.0 282.9 jit_solution(1578596560247495090)
XLA Ops:
  8.8 1.8 collective-permute-start.1
  10.6 2.4 collective-permute-start.2
  13.0 2.4 collective-permute-start.3
  17.3 1.4 collective-permute-start.5
  18.6 1.3 collective-permute-start.6
  19.9 1.5 collective-permute-start.7
  21.6 2.7 collective-permute-start.9
  24.3 1.5 collective-permute-start.10
  25.8 1.7 collective-permute-start.11
  27.5 2.1 collective-permute-start.12
  30.7 1.2 collective-permute-done.10
  31.9 10.3 %collective-permute-start.23 = (bf16[256,512]{1,0:T(8,128)(2,1)}, bf16[256,512]{1,0:T(8,128)(2,1)S(1)}, u32[]{:S(2)}, u32[]{:S(2)}) collective-permute-start(bf16[256,512]{1,0:T(8,128)(2,1)} %param.13), channel_id=1, source_target_pairs={{0,0},{1,16},{2,32},{3,48},{4,64},{5,80},{6,96},{7,112},{8,128},{9... | collective-permute-start | bytes 786440 | tf_op jit(solution)/shard_map/ppermute | solution.py:112
  42.3 1.8 collective-permute-done.13
  44.8 6.2 %fusion.23 = bf16[512,64]{0,1:T(8,128)(2,1)S(1)} fusion(bf16[512,8192]{1,0:T(8,128)(2,1)} %param.8, bf16[8192,64]{0,1:T(8,128)(2,1)S(1)} %bitcast.100, pred[8192]{0:T(1024)(128)(4,1)S(1)} %bitcast.113), kind=kOutput, calls=%fused_computation.23 | convolution fusion | flops 537427968 | bytes 9510912 | tf_op jit(solution)/shard_map/dot_general | solution.py:55
  52.4 15.2 %all-to-all-start = ((bf16[16,512,2,8]{1,3,2,0:T(8,128)(2,1)}), bf16[16,512,2,8]{1,3,2,0:T(8,128)(2,1)S(1)}, u32[]{:S(2)}, u32[]{:S(2)}) async-start(bf16[16,512,2,8]{1,3,2,0:T(8,128)(2,1)} %broadcast_select_fusion), calls=%async_computation | async-start | bytes 524288 | tf_op jit(solution)/shard_map/all_to_all | solution.py:66
  67.8 1.3 multiply_cosine_fusion.1
  69.0 11.6 %all-to-all-done = bf16[16,512,2,8]{1,3,2,0:T(8,128)(2,1)S(1)} async-done(((bf16[16,512,2,8]{1,3,2,0:T(8,128)(2,1)}), bf16[16,512,2,8]{1,3,2,0:T(8,128)(2,1)S(1)}, u32[]{:S(2)}, u32[]{:S(2)}) %all-to-all-start) | async-done | bytes 262176 | tf_op jit(solution)/shard_map/all_to_all | solution.py:66
  81.3 1.3 collective-permute-start.15
  83.3 1.3 collective-permute-start.16
  84.7 1.9 collective-permute-start.17
  87.5 1.9 collective-permute-start.18
  89.4 2.7 collective-permute-start.19
  92.1 2.0 collective-permute-start.20
  94.9 2.0 collective-permute-start.21
  97.0 9.4 %collective-permute-done.17 = bf16[512,256]{0,1:T(8,128)(2,1)S(1)} collective-permute-done((bf16[512,256]{0,1:T(8,128)(2,1)S(1)}, bf16[512,256]{0,1:T(8,128)(2,1)S(1)}, u32[]{:S(2)}, u32[]{:S(2)}) %collective-permute-start.17) | collective-permute-done | bytes 262176 | tf_op jit(solution)/shard_map/ppermute | solution.py:79
  106.4 1.9 collective-permute-start.22
  108.3 5.3 %collective-permute-done.18 = bf16[512,256]{0,1:T(8,128)(2,1)S(1)} collective-permute-done((bf16[512,256]{0,1:T(8,128)(2,1)S(1)}, bf16[512,256]{0,1:T(8,128)(2,1)S(1)}, u32[]{:S(2)}, u32[]{:S(2)}) %collective-permute-start.18) | collective-permute-done | bytes 262176 | tf_op jit(solution)/shard_map/ppermute | solution.py:79
  113.6 11.2 %collective-permute-done.19 = bf16[512,256]{0,1:T(8,128)(2,1)S(1)} collective-permute-done((bf16[512,256]{0,1:T(8,128)(2,1)S(1)}, bf16[512,256]{0,1:T(8,128)(2,1)S(1)}, u32[]{:S(2)}, u32[]{:S(2)}) %collective-permute-start.19) | collective-permute-done | bytes 262176 | tf_op jit(solution)/shard_map/ppermute | solution.py:79
  124.8 11.4 %collective-permute-done.20 = bf16[512,256]{0,1:T(8,128)(2,1)S(1)} collective-permute-done((bf16[512,256]{0,1:T(8,128)(2,1)S(1)}, bf16[512,256]{0,1:T(8,128)(2,1)S(1)}, u32[]{:S(2)}, u32[]{:S(2)}) %collective-permute-start.20) | collective-permute-done | bytes 262176 | tf_op jit(solution)/shard_map/ppermute | solution.py:79
  136.2 6.4 %collective-permute-done.21 = bf16[512,256]{0,1:T(8,128)(2,1)S(1)} collective-permute-done((bf16[512,256]{0,1:T(8,128)(2,1)S(1)}, bf16[512,256]{0,1:T(8,128)(2,1)S(1)}, u32[]{:S(2)}, u32[]{:S(2)}) %collective-permute-start.21) | collective-permute-done | bytes 262176 | tf_op jit(solution)/shard_map/ppermute | solution.py:79
  144.5 7.0 %fusion.43 = f32[512,256]{0,1:T(8,128)S(1)} fusion(bf16[512,8192]{1,0:T(8,128)(2,1)} %param.8, bf16[8192,256]{1,0:T(8,128)(2,1)} %all-gather.4.cloned.1.call-done), kind=kOutput, calls=%fused_computation.114 | convolution fusion | flops 2147483648 | bytes 13107200 | tf_op jit(solution)/shard_map/dot_general | solution.py:57
  151.9 17.3 %while.11 = (s32[]{:T(128)}, bf16[4,256,128]{2,1,0:T(8,128)(2,1)S(1)}, s32[4,256]{1,0:T(4,128)S(1)}, s32[4608]{0:T(1024)S(1)}, s32[4,256]{1,0:T(4,128)S(1)}, /*i...) while((s32[]{:T(128)}, ...), condition=%wide.region_6.7_spmd.clone, body=%wide.region_3.6_spmd.clone.sunk | while | flops 625283072 | bytes 16798836 | solution.py:109
  151.9 1.4 fusion.61
  153.3 1.5 fusion.62
  154.7 1.5 fusion.63
  156.2 1.4 fusion.61
  157.6 1.5 fusion.62
  159.0 1.5 fusion.63
  160.5 1.4 fusion.61
  161.9 1.5 fusion.62
  163.3 1.5 fusion.63
  164.9 1.4 fusion.61
  166.2 1.5 fusion.62
  167.7 1.5 fusion.63
  169.1 0.9 copy.31
  170.0 74.1 %all-gather.6.cloned.1.call-done = bf16[512,4096]{0,1:T(8,128)(2,1)} async-done(((bf16[512,256]{0,1:T(8,128)(2,1)}), bf16[512,4096]{0,1:T(8,128)(2,1)}) %all-gather.6.cloned.1.call-update) | async-done | bytes 4194320 | tf_op jit(solution)/shard_map/all_gather | solution.py:118
  244.2 5.8 %convolution_convert_fusion = bf16[512,512]{1,0:T(8,128)(2,1)S(1)} fusion(bf16[512,4096]{0,1:T(8,128)(2,1)} %all-gather.6.cloned.1.call-done, bf16[4096,512]{1,0:T(8,128)(2,1)} %all-gather.8.cloned.1.call-done), kind=kOutput, calls=%fused_computation.21 | convolution fusion | flops 2147745792 | bytes 8912896 | tf_op jit(solution)/shard_map/dot_general | solution.py:119
  250.0 25.6 %all_to_all.10 = bf16[16,32,512]{2,1,0:T(8,128)(2,1)S(1)} all-to-all(bf16[16,32,512]{2,1,0:T(8,128)(2,1)S(1)} %bitcast.104), channel_id=1, replica_groups=mesh['ctx'=16,'tp'=16] {'tp'}, dimensions={0} | all-to-all | bytes 1048576 | tf_op jit(solution)/shard_map/all_to_all | solution.py:125
  (116 shorter events, 13.6 us)
Async XLA Ops:
  6.5 137.9 %all-gather.4.cloned.1.call-start = ((), (), s32[]{:S(2)}) async-start(), calls=%async_computation.2 | async-start | bytes 4456448 | tf_op jit(solution)/shard_map/all_gather | solution.py:56
  8.8 8.5 %collective-permute-start = (bf16[512,64]{0,1:T(8,128)(2,1)S(1)}, bf16[512,64]{0,1:T(8,128)(2,1)S(1)}, u32[]{:S(2)}, u32[]{:S(2)}) collective-permute-start(bf16[512,64]{0,1:T(8,128)(2,1)S(1)} %constant_dynamic-update-slice_fusion), channel_id=1, source_target_pairs={{0,16},{16,32},{32,48},{48,64},{64,80},{80,96},{96,112},{112,128},... | collective-permute-start | bytes 196616 | tf_op jit(solution)/shard_map/ppermute | solution.py:50
  8.8 9.8 %collective-permute-start.1 = (bf16[512,64]{0,1:T(8,128)(2,1)S(1)}, bf16[512,64]{0,1:T(8,128)(2,1)S(1)}, u32[]{:S(2)}, u32[]{:S(2)}) collective-permute-start(bf16[512,64]{0,1:T(8,128)(2,1)S(1)} %constant_dynamic-update-slice_fusion), channel_id=1, source_target_pairs={{0,32},{16,48},{32,64},{48,80},{64,96},{80,112},{96,128},{112,144}... | collective-permute-start | bytes 196616 | tf_op jit(solution)/shard_map/ppermute | solution.py:50
  10.6 9.3 %collective-permute-start.2 = (bf16[512,64]{0,1:T(8,128)(2,1)S(1)}, bf16[512,64]{0,1:T(8,128)(2,1)S(1)}, u32[]{:S(2)}, u32[]{:S(2)}) collective-permute-start(bf16[512,64]{0,1:T(8,128)(2,1)S(1)} %constant_dynamic-update-slice_fusion), channel_id=1, source_target_pairs={{0,48},{16,64},{32,80},{48,96},{64,112},{80,128},{96,144},{112,160... | collective-permute-start | bytes 196616 | tf_op jit(solution)/shard_map/ppermute | solution.py:50
  13.0 8.4 %collective-permute-start.3 = (bf16[512,64]{0,1:T(8,128)(2,1)S(1)}, bf16[512,64]{0,1:T(8,128)(2,1)S(1)}, u32[]{:S(2)}, u32[]{:S(2)}) collective-permute-start(bf16[512,64]{0,1:T(8,128)(2,1)S(1)} %constant_dynamic-update-slice_fusion), channel_id=1, source_target_pairs={{0,64},{16,80},{32,96},{48,112},{64,128},{80,144},{96,160},{112,17... | collective-permute-start | bytes 196616 | tf_op jit(solution)/shard_map/ppermute | solution.py:50
  15.4 6.2 %collective-permute-start.4 = (bf16[512,64]{0,1:T(8,128)(2,1)S(1)}, bf16[512,64]{0,1:T(8,128)(2,1)S(1)}, u32[]{:S(2)}, u32[]{:S(2)}) collective-permute-start(bf16[512,64]{0,1:T(8,128)(2,1)S(1)} %constant_dynamic-update-slice_fusion), channel_id=1, source_target_pairs={{0,80},{16,96},{32,112},{48,128},{64,144},{80,160},{96,176},{112,1... | collective-permute-start | bytes 196616 | tf_op jit(solution)/shard_map/ppermute | solution.py:50
  17.3 7.1 %collective-permute-start.5 = (bf16[512,64]{0,1:T(8,128)(2,1)S(1)}, bf16[512,64]{0,1:T(8,128)(2,1)S(1)}, u32[]{:S(2)}, u32[]{:S(2)}) collective-permute-start(bf16[512,64]{0,1:T(8,128)(2,1)S(1)} %constant_dynamic-update-slice_fusion), channel_id=1, source_target_pairs={{0,96},{16,112},{32,128},{48,144},{64,160},{80,176},{96,192},{112,... | collective-permute-start | bytes 196616 | tf_op jit(solution)/shard_map/ppermute | solution.py:50
  18.6 7.2 %collective-permute-start.6 = (bf16[512,64]{0,1:T(8,128)(2,1)S(1)}, bf16[512,64]{0,1:T(8,128)(2,1)S(1)}, u32[]{:S(2)}, u32[]{:S(2)}) collective-permute-start(bf16[512,64]{0,1:T(8,128)(2,1)S(1)} %constant_dynamic-update-slice_fusion), channel_id=1, source_target_pairs={{0,112},{16,128},{32,144},{48,160},{64,176},{80,192},{96,208},{112... | collective-permute-start | bytes 196616 | tf_op jit(solution)/shard_map/ppermute | solution.py:50
  19.9 7.6 %collective-permute-start.7 = (bf16[512,64]{0,1:T(8,128)(2,1)S(1)}, bf16[512,64]{0,1:T(8,128)(2,1)S(1)}, u32[]{:S(2)}, u32[]{:S(2)}) collective-permute-start(bf16[512,64]{0,1:T(8,128)(2,1)S(1)} %constant_dynamic-update-slice_fusion), channel_id=1, source_target_pairs={{0,128},{16,144},{32,160},{48,176},{64,192},{80,208},{96,224},{112... | collective-permute-start | bytes 196616 | tf_op jit(solution)/shard_map/ppermute | solution.py:50
  21.5 8.2 %collective-permute-start.8 = (bf16[512,64]{0,1:T(8,128)(2,1)S(1)}, bf16[512,64]{0,1:T(8,128)(2,1)S(1)}, u32[]{:S(2)}, u32[]{:S(2)}) collective-permute-start(bf16[512,64]{0,1:T(8,128)(2,1)S(1)} %constant_dynamic-update-slice_fusion), channel_id=1, source_target_pairs={{0,144},{16,160},{32,176},{48,192},{64,208},{80,224},{96,240},{112... | collective-permute-start | bytes 196616 | tf_op jit(solution)/shard_map/ppermute | solution.py:50
  21.6 8.4 %collective-permute-start.9 = (bf16[512,64]{0,1:T(8,128)(2,1)S(1)}, bf16[512,64]{0,1:T(8,128)(2,1)S(1)}, u32[]{:S(2)}, u32[]{:S(2)}) collective-permute-start(bf16[512,64]{0,1:T(8,128)(2,1)S(1)} %constant_dynamic-update-slice_fusion), channel_id=1, source_target_pairs={{0,160},{16,176},{32,192},{48,208},{64,224},{80,240},{96,0},{112,1... | collective-permute-start | bytes 196616 | tf_op jit(solution)/shard_map/ppermute | solution.py:50
  24.3 7.6 %collective-permute-start.10 = (bf16[512,64]{0,1:T(8,128)(2,1)S(1)}, bf16[512,64]{0,1:T(8,128)(2,1)S(1)}, u32[]{:S(2)}, u32[]{:S(2)}) collective-permute-start(bf16[512,64]{0,1:T(8,128)(2,1)S(1)} %constant_dynamic-update-slice_fusion), channel_id=1, source_target_pairs={{0,176},{16,192},{32,208},{48,224},{64,240},{80,0},{96,16},{112,32... | collective-permute-start | bytes 196616 | tf_op jit(solution)/shard_map/ppermute | solution.py:50
  25.8 16.4 %collective-permute-start.11 = (bf16[512,64]{0,1:T(8,128)(2,1)S(1)}, bf16[512,64]{0,1:T(8,128)(2,1)S(1)}, u32[]{:S(2)}, u32[]{:S(2)}) collective-permute-start(bf16[512,64]{0,1:T(8,128)(2,1)S(1)} %constant_dynamic-update-slice_fusion), channel_id=1, source_target_pairs={{0,192},{16,208},{32,224},{48,240},{64,0},{80,16},{96,32},{112,48}... | collective-permute-start | bytes 196616 | tf_op jit(solution)/shard_map/ppermute | solution.py:50
  27.5 14.8 %collective-permute-start.12 = (bf16[512,64]{0,1:T(8,128)(2,1)S(1)}, bf16[512,64]{0,1:T(8,128)(2,1)S(1)}, u32[]{:S(2)}, u32[]{:S(2)}) collective-permute-start(bf16[512,64]{0,1:T(8,128)(2,1)S(1)} %constant_dynamic-update-slice_fusion), channel_id=1, source_target_pairs={{0,208},{16,224},{32,240},{48,0},{64,16},{80,32},{96,48},{112,64},... | collective-permute-start | bytes 196616 | tf_op jit(solution)/shard_map/ppermute | solution.py:50
  29.6 14.4 %collective-permute-start.13 = (bf16[512,64]{0,1:T(8,128)(2,1)S(1)}, bf16[512,64]{0,1:T(8,128)(2,1)S(1)}, u32[]{:S(2)}, u32[]{:S(2)}) collective-permute-start(bf16[512,64]{0,1:T(8,128)(2,1)S(1)} %constant_dynamic-update-slice_fusion), channel_id=1, source_target_pairs={{0,224},{16,240},{32,0},{48,16},{64,32},{80,48},{96,64},{112,80},{... | collective-permute-start | bytes 196616 | tf_op jit(solution)/shard_map/ppermute | solution.py:50
  30.0 14.1 %collective-permute-start.14 = (bf16[512,64]{0,1:T(8,128)(2,1)S(1)}, bf16[512,64]{0,1:T(8,128)(2,1)S(1)}, u32[]{:S(2)}, u32[]{:S(2)}) collective-permute-start(bf16[512,64]{0,1:T(8,128)(2,1)S(1)} %constant_dynamic-update-slice_fusion), channel_id=1, source_target_pairs={{0,240},{16,0},{32,16},{48,32},{64,48},{80,64},{96,80},{112,96},{1... | collective-permute-start | bytes 196616 | tf_op jit(solution)/shard_map/ppermute | solution.py:50
  31.9 54.7 %collective-permute-start.23 = (bf16[256,512]{1,0:T(8,128)(2,1)}, bf16[256,512]{1,0:T(8,128)(2,1)S(1)}, u32[]{:S(2)}, u32[]{:S(2)}) collective-permute-start(bf16[256,512]{1,0:T(8,128)(2,1)} %param.13), channel_id=1, source_target_pairs={{0,0},{1,16},{2,32},{3,48},{4,64},{5,80},{6,96},{7,112},{8,128},{9... | collective-permute-start | bytes 786440 | tf_op jit(solution)/shard_map/ppermute | solution.py:112
  52.4 28.3 %all-to-all-start = ((bf16[16,512,2,8]{1,3,2,0:T(8,128)(2,1)}), bf16[16,512,2,8]{1,3,2,0:T(8,128)(2,1)S(1)}, u32[]{:S(2)}, u32[]{:S(2)}) async-start(bf16[16,512,2,8]{1,3,2,0:T(8,128)(2,1)} %broadcast_select_fusion), calls=%async_computation | async-start | bytes 524288 | tf_op jit(solution)/shard_map/all_to_all | solution.py:66
  67.6 102.5 %all-gather.8.cloned.1.call-start = ((), (), s32[]{:S(2)}) async-start(), calls=%async_computation.4 | async-start | bytes 4456448 | tf_op jit(solution)/shard_map/all_gather | solution.py:117
  81.3 10.8 %collective-permute-start.15 = (bf16[512,256]{0,1:T(8,128)(2,1)S(1)}, bf16[512,256]{0,1:T(8,128)(2,1)S(1)}, u32[]{:S(2)}, u32[]{:S(2)}) collective-permute-start(bf16[512,256]{0,1:T(8,128)(2,1)S(1)} %pad_maximum_fusion), channel_id=1, source_target_pairs={{0,128},{16,144},{32,160},{48,176},{64,192},{80,208},{96,224},{112... | collective-permute-start | bytes 786440 | tf_op jit(solution)/shard_map/ppermute | solution.py:79
  83.3 11.7 %collective-permute-start.16 = (bf16[512,256]{0,1:T(8,128)(2,1)S(1)}, bf16[512,256]{0,1:T(8,128)(2,1)S(1)}, u32[]{:S(2)}, u32[]{:S(2)}) collective-permute-start(bf16[512,256]{0,1:T(8,128)(2,1)S(1)} %pad_maximum_fusion), channel_id=1, source_target_pairs={{0,112},{16,128},{32,144},{48,160},{64,176},{80,192},{96,208},{112... | collective-permute-start | bytes 786440 | tf_op jit(solution)/shard_map/ppermute | solution.py:79
  84.7 21.7 %collective-permute-start.17 = (bf16[512,256]{0,1:T(8,128)(2,1)S(1)}, bf16[512,256]{0,1:T(8,128)(2,1)S(1)}, u32[]{:S(2)}, u32[]{:S(2)}) collective-permute-start(bf16[512,256]{0,1:T(8,128)(2,1)S(1)} %pad_maximum_fusion), channel_id=1, source_target_pairs={{0,96},{16,112},{32,128},{48,144},{64,160},{80,176},{96,192},{112,... | collective-permute-start | bytes 786440 | tf_op jit(solution)/shard_map/ppermute | solution.py:79
  86.7 0.7 copy-start.3
  87.4 156.7 %all-gather.6.cloned.1.call-start = ((), (), s32[]{:S(2)}) async-start(), calls=%async_computation.3 | async-start | bytes 4456448 | tf_op jit(solution)/shard_map/all_gather | solution.py:118
  87.5 26.1 %collective-permute-start.18 = (bf16[512,256]{0,1:T(8,128)(2,1)S(1)}, bf16[512,256]{0,1:T(8,128)(2,1)S(1)}, u32[]{:S(2)}, u32[]{:S(2)}) collective-permute-start(bf16[512,256]{0,1:T(8,128)(2,1)S(1)} %pad_maximum_fusion), channel_id=1, source_target_pairs={{0,80},{16,96},{32,112},{48,128},{64,144},{80,160},{96,176},{112,1... | collective-permute-start | bytes 786440 | tf_op jit(solution)/shard_map/ppermute | solution.py:79
  89.4 35.4 %collective-permute-start.19 = (bf16[512,256]{0,1:T(8,128)(2,1)S(1)}, bf16[512,256]{0,1:T(8,128)(2,1)S(1)}, u32[]{:S(2)}, u32[]{:S(2)}) collective-permute-start(bf16[512,256]{0,1:T(8,128)(2,1)S(1)} %pad_maximum_fusion), channel_id=1, source_target_pairs={{0,64},{16,80},{32,96},{48,112},{64,128},{80,144},{96,160},{112,17... | collective-permute-start | bytes 786440 | tf_op jit(solution)/shard_map/ppermute | solution.py:79
  92.1 44.1 %collective-permute-start.20 = (bf16[512,256]{0,1:T(8,128)(2,1)S(1)}, bf16[512,256]{0,1:T(8,128)(2,1)S(1)}, u32[]{:S(2)}, u32[]{:S(2)}) collective-permute-start(bf16[512,256]{0,1:T(8,128)(2,1)S(1)} %pad_maximum_fusion), channel_id=1, source_target_pairs={{0,48},{16,64},{32,80},{48,96},{64,112},{80,128},{96,144},{112,160... | collective-permute-start | bytes 786440 | tf_op jit(solution)/shard_map/ppermute | solution.py:79
  94.9 47.8 %collective-permute-start.21 = (bf16[512,256]{0,1:T(8,128)(2,1)S(1)}, bf16[512,256]{0,1:T(8,128)(2,1)S(1)}, u32[]{:S(2)}, u32[]{:S(2)}) collective-permute-start(bf16[512,256]{0,1:T(8,128)(2,1)S(1)} %pad_maximum_fusion), channel_id=1, source_target_pairs={{0,32},{16,48},{32,64},{48,80},{64,96},{80,112},{96,128},{112,144}... | collective-permute-start | bytes 786440 | tf_op jit(solution)/shard_map/ppermute | solution.py:79
  106.4 36.3 %collective-permute-start.22 = (bf16[512,256]{0,1:T(8,128)(2,1)S(1)}, bf16[512,256]{0,1:T(8,128)(2,1)S(1)}, u32[]{:S(2)}, u32[]{:S(2)}) collective-permute-start(bf16[512,256]{0,1:T(8,128)(2,1)S(1)} %pad_maximum_fusion), channel_id=1, source_target_pairs={{0,16},{16,32},{32,48},{48,64},{64,80},{80,96},{96,112},{112,128},... | collective-permute-start | bytes 786440 | tf_op jit(solution)/shard_map/ppermute | solution.py:79
  144.4 7.1 %copy-start.1 = (f32[512,64]{0,1:T(8,128)S(1)}, f32[512,64]{0,1:T(8,128)}, u32[]{:S(2)}) copy-start(f32[512,64]{0,1:T(8,128)} %get-tuple-element.131) | copy-start | bytes 393220
  144.4 7.1 %copy-start.2 = (f32[512,64]{0,1:T(8,128)S(1)}, f32[512,64]{0,1:T(8,128)}, u32[]{:S(2)}) copy-start(f32[512,64]{0,1:T(8,128)} %get-tuple-element.132) | copy-start | bytes 393220
  144.4 7.4 %copy-start = (s32[4608]{0:T(1024)S(1)}, s32[4608]{0:T(1024)}, u32[]{:S(2)}) copy-start(s32[4608]{0:T(1024)} %compare_select_fusion) | copy-start | bytes 55300
  144.4 7.4 %copy-start.4 = (bf16[4,256,128]{2,1,0:T(8,128)(2,1)S(1)}, bf16[4,256,128]{2,1,0:T(8,128)(2,1)}, u32[]{:S(2)}) copy-start(bf16[4,256,128]{2,1,0:T(8,128)(2,1)} %custom-call.7) | copy-start | bytes 786436
Sparse Core Ops, SparseCore 0:
  9.2 57.2 all-gather.3
  87.5 52.1 all-gather.7
  170.1 73.9 all-gather.5
where the time goes:
time: 284 us; the launch traced here: 283 us
  waiting for transfers between devices  134 us (47%)
  starting transfers between devices  60.7 us (21%)
  matrix products  30.3 us (11%)
  blocking collectives  25.6 us (9%)
  between operations  13.7 us (5%)
  other arithmetic  11.1 us (4%)
  local copies, waits for them, and re-layouts  7.47 us (3%)
    all_gather x1, waiting for transfers between devices, on_device(): attended_all = lax.all_gather(attended, 'tp', axis=1, tiled=True)  74.1 us
    ppermute x8, waiting for transfers between devices, on_device(): lax.ppermute(kv_rows_local, 'ctx', [(i, i + shift) for i in range(n_ctx -...  44.5 us
    all_to_all x1, blocking collectives, on_device(): got_rows = lax.all_to_all(sent, 'tp', 0, 0, tiled=False)  25.6 us
    ppermute x15, starting transfers between devices, on_device(): lax.ppermute(w_kv, 'ctx', [(i, (i + shift) % n_ctx_all) for i in range(n_...  20.1 us
    all_to_all x1, starting transfers between devices, on_device(): got = lax.all_to_all(pieces, 'tp', 0, 0, tiled=False)  15.2 us
    ppermute x8, starting transfers between devices, on_device(): lax.ppermute(kv_rows_local, 'ctx', [(i, i + shift) for i in range(n_ctx -...  15 us
    all_to_all x1, waiting for transfers between devices, on_device(): got = lax.all_to_all(pieces, 'tp', 0, 0, tiled=False)  11.6 us
    ppermute x1, starting transfers between devices, on_device(): lax.ppermute(w_output, ('ctx', 'tp'), [(c * n_tp + t, t * n_tp + c) for c...  10.3 us
  transfers between devices with their start and end apart: 28, of which 10 were waited for; matrix products, arithmetic and copies ran while one was open for 15% of the time, Pallas kernels for 0%

commit v1 on v0

--- a/solution.py
+++ b/solution.py
@@ -8,6 +8,12 @@
 KVH = 4
 DOC_MOST = 4096
 rope_base = 500000.0
+
+
+def meet_links_now(mat):
+    return jnp.concatenate(
+        lax.all_to_all(jnp.stack(lax.psum(1, "tp") * [mat], axis=0), "tp", 0, 0), axis=1
+    )
 
 
 def rotate(field, positions):
@@ -115,7 +121,7 @@
         [(c * n_tp + t, t * n_tp + c) for c in range(n_ctx_all) for t in range(n_tp)],
     )
     w_chunk = lax.all_gather(w_moved, "ctx", axis=0, tiled=True)
-    attended_all = lax.all_gather(attended, "tp", axis=1, tiled=True)
+    attended_all = meet_links_now(attended)
     out_chunk = jnp.dot(attended_all, w_chunk, preferred_element_type=jnp.float32).astype(
         jnp.bfloat16
     )

time: 284 us -> 307 us (1.081)
  the two profiles are of different devices: /device:TPU:6 before, /device:TPU:32 now
where the time goes in v1:
time: 307 us; the launch traced here: 306 us
  waiting for transfers between devices  151 us (49%)
  starting transfers between devices  65.7 us (21%)
  matrix products  30.3 us (10%)
  blocking collectives  24.4 us (8%)
  between operations  14 us (5%)
  other arithmetic  11 us (4%)
  local copies, waits for them, and re-layouts  9.17 us (3%)
    all_to_all x1, waiting for transfers between devices, meet_links_now(): lax.all_to_all(jnp.stack(lax.psum(1, 'tp') * [mat], axis=0), 'tp', 0, 0)  86.8 us
    ppermute x8, waiting for transfers between devices, on_device(): lax.ppermute(kv_rows_local, 'ctx', [(i, i + shift) for i in range(n_ctx -...  50.5 us
    all_to_all x1, blocking collectives, on_device(): got_rows = lax.all_to_all(sent, 'tp', 0, 0, tiled=False)  24.4 us
    ppermute x15, starting transfers between devices, on_device(): lax.ppermute(w_kv, 'ctx', [(i, (i + shift) % n_ctx_all) for i in range(n_...  22 us
    ppermute x8, starting transfers between devices, on_device(): lax.ppermute(kv_rows_local, 'ctx', [(i, i + shift) for i in range(n_ctx -...  16.3 us
    all_to_all x1, starting transfers between devices, on_device(): got = lax.all_to_all(pieces, 'tp', 0, 0, tiled=False)  14.4 us
    all_to_all x1, waiting for transfers between devices, on_device(): got = lax.all_to_all(pieces, 'tp', 0, 0, tiled=False)  10.3 us
    ppermute x1, starting transfers between devices, on_device(): lax.ppermute(w_output, ('ctx', 'tp'), [(c * n_tp + t, t * n_tp + c) for c...  8.47 us
  transfers between devices with their start and end apart: 28, of which 9 were waited for; matrix products, arithmetic and copies ran while one was open for 14% of the time, Pallas kernels for 0%

profile of v1, /device:TPU:32, one launch (start us, length us, event | category | flops | bytes accessed | tf_op | source)
XLA Modules:
  0.0 305.9 jit_solution(8241838994931125718)
XLA Ops:
  8.8 1.5 collective-permute-start.1
  10.3 2.1 collective-permute-start.2
  12.4 2.1 collective-permute-start.3
  17.2 2.9 collective-permute-start.5
  20.2 1.5 collective-permute-start.7
  22.2 1.8 collective-permute-start.9
  24.0 1.8 collective-permute-start.10
  25.8 2.5 collective-permute-start.11
  28.3 1.2 collective-permute-start.12
  29.6 2.4 collective-permute-start.13
  33.3 8.5 %collective-permute-start.23 = (bf16[256,512]{1,0:T(8,128)(2,1)}, bf16[256,512]{1,0:T(8,128)(2,1)S(1)}, u32[]{:S(2)}, u32[]{:S(2)}) collective-permute-start(bf16[256,512]{1,0:T(8,128)(2,1)} %param.13), channel_id=1, source_target_pairs={{0,0},{1,16},{2,32},{3,48},{4,64},{5,80},{6,96},{7,112},{8,128},{9... | collective-permute-start | bytes 786440 | tf_op jit(solution)/shard_map/ppermute | solution.py:118
  41.9 2.0 collective-permute-done.14
  44.6 6.2 %fusion.23 = bf16[512,64]{0,1:T(8,128)(2,1)S(1)} fusion(bf16[512,8192]{1,0:T(8,128)(2,1)} %param.8, bf16[8192,64]{0,1:T(8,128)(2,1)S(1)} %bitcast.103, pred[8192]{0:T(1024)(128)(4,1)S(1)} %bitcast.116), kind=kOutput, calls=%fused_computation.23 | convolution fusion | flops 537427968 | bytes 9510912 | tf_op jit(solution)/shard_map/dot_general | solution.py:61
  52.2 14.4 %all-to-all-start = ((bf16[16,512,2,8]{1,3,2,0:T(8,128)(2,1)}), bf16[16,512,2,8]{1,3,2,0:T(8,128)(2,1)S(1)}, u32[]{:S(2)}, u32[]{:S(2)}) async-start(bf16[16,512,2,8]{1,3,2,0:T(8,128)(2,1)} %broadcast_select_fusion), calls=%async_computation | async-start | bytes 524288 | tf_op jit(solution)/shard_map/all_to_all | solution.py:72
  66.8 1.3 multiply_cosine_fusion.1
  68.0 10.3 %all-to-all-done = bf16[16,512,2,8]{1,3,2,0:T(8,128)(2,1)S(1)} async-done(((bf16[16,512,2,8]{1,3,2,0:T(8,128)(2,1)}), bf16[16,512,2,8]{1,3,2,0:T(8,128)(2,1)S(1)}, u32[]{:S(2)}, u32[]{:S(2)}) %all-to-all-start) | async-done | bytes 262176 | tf_op jit(solution)/shard_map/all_to_all | solution.py:72
  79.1 1.3 collective-permute-start.15
  81.0 3.5 %collective-permute-start.16 = (bf16[512,256]{0,1:T(8,128)(2,1)S(1)}, bf16[512,256]{0,1:T(8,128)(2,1)S(1)}, u32[]{:S(2)}, u32[]{:S(2)}) collective-permute-start(bf16[512,256]{0,1:T(8,128)(2,1)S(1)} %pad_maximum_fusion), channel_id=1, source_target_pairs={{0,112},{16,128},{32,144},{48,160},{64,176},{80,192},{96,208},{112... | collective-permute-start | bytes 786440 | tf_op jit(solution)/shard_map/ppermute | solution.py:85
  84.6 1.9 collective-permute-start.17
  87.3 1.9 collective-permute-start.18
  89.2 1.9 collective-permute-start.19
  91.2 1.9 collective-permute-start.20
  93.2 1.9 collective-permute-start.21
  95.1 2.2 collective-permute-done.17
  97.3 1.9 collective-permute-start.22
  99.3 7.5 %collective-permute-done.19 = bf16[512,256]{0,1:T(8,128)(2,1)S(1)} collective-permute-done((bf16[512,256]{0,1:T(8,128)(2,1)S(1)}, bf16[512,256]{0,1:T(8,128)(2,1)S(1)}, u32[]{:S(2)}, u32[]{:S(2)}) %collective-permute-start.19) | collective-permute-done | bytes 262176 | tf_op jit(solution)/shard_map/ppermute | solution.py:85
  106.8 11.2 %collective-permute-done.20 = bf16[512,256]{0,1:T(8,128)(2,1)S(1)} collective-permute-done((bf16[512,256]{0,1:T(8,128)(2,1)S(1)}, bf16[512,256]{0,1:T(8,128)(2,1)S(1)}, u32[]{:S(2)}, u32[]{:S(2)}) %collective-permute-start.20) | collective-permute-done | bytes 262176 | tf_op jit(solution)/shard_map/ppermute | solution.py:85
  118.1 27.4 %collective-permute-done.21 = bf16[512,256]{0,1:T(8,128)(2,1)S(1)} collective-permute-done((bf16[512,256]{0,1:T(8,128)(2,1)S(1)}, bf16[512,256]{0,1:T(8,128)(2,1)S(1)}, u32[]{:S(2)}, u32[]{:S(2)}) %collective-permute-start.21) | collective-permute-done | bytes 262176 | tf_op jit(solution)/shard_map/ppermute | solution.py:85
  145.5 2.2 collective-permute-done.22
  149.4 7.0 %fusion.43 = f32[512,256]{0,1:T(8,128)S(1)} fusion(bf16[512,8192]{1,0:T(8,128)(2,1)} %param.8, bf16[8192,256]{1,0:T(8,128)(2,1)} %all-gather.3.cloned.1.call-done), kind=kOutput, calls=%fused_computation.114 | convolution fusion | flops 2147483648 | bytes 13107200 | tf_op jit(solution)/shard_map/dot_general | solution.py:63
  156.8 17.3 %while.11 = (s32[]{:T(128)}, bf16[4,256,128]{2,1,0:T(8,128)(2,1)S(1)}, s32[4,256]{1,0:T(4,128)S(1)}, s32[4608]{0:T(1024)S(1)}, s32[4,256]{1,0:T(4,128)S(1)}, /*i...) while((s32[]{:T(128)}, ...), condition=%wide.region_6.7_spmd.clone, body=%wide.region_3.6_spmd.clone.sunk | while | flops 625283072 | bytes 16798836 | solution.py:115
  156.9 1.4 fusion.61
  158.2 1.5 fusion.62
  159.7 1.5 fusion.63
  161.2 1.4 fusion.61
  162.5 1.5 fusion.62
  164.0 1.5 fusion.63
  165.5 1.4 fusion.61
  166.9 1.5 fusion.62
  168.3 1.5 fusion.63
  169.8 1.4 fusion.61
  171.2 1.5 fusion.62
  172.6 1.5 fusion.63
  174.3 2.4 stack.71
  176.7 4.5 %all-to-all-start.1 = ((bf16[16,512,256]{1,2,0:T(8,128)(2,1)}), bf16[16,512,256]{1,2,0:T(8,128)(2,1)}, u32[]{:S(2)}, u32[]{:S(2)}) async-start(bf16[16,512,256]{1,2,0:T(8,128)(2,1)} %stack.71), calls=%async_computation.1 | async-start | bytes 8388608 | tf_op jit(solution)/shard_map/all_to_all | solution.py:15
  181.2 86.8 %all-to-all-done.1 = bf16[16,512,256]{1,2,0:T(8,128)(2,1)} async-done(((bf16[16,512,256]{1,2,0:T(8,128)(2,1)}), bf16[16,512,256]{1,2,0:T(8,128)(2,1)}, u32[]{:S(2)}, u32[]{:S(2)}) %all-to-all-start.1) | async-done | bytes 4194336 | tf_op jit(solution)/shard_map/all_to_all | solution.py:15
  268.0 5.8 %convolution_convert_fusion = bf16[512,512]{1,0:T(8,128)(2,1)S(1)} fusion(bf16[512,4096]{0,1:T(8,128)(2,1)} %bitcast.32, bf16[4096,512]{1,0:T(8,128)(2,1)} %all-gather.5.cloned.1.call-done), kind=kOutput, calls=%fused_computation.21 | convolution fusion | flops 2147745792 | bytes 8912896 | tf_op jit(solution)/shard_map/dot_general | solution.py:125
  273.8 24.4 %all_to_all.15 = bf16[16,32,512]{2,1,0:T(8,128)(2,1)S(1)} all-to-all(bf16[16,32,512]{2,1,0:T(8,128)(2,1)S(1)} %bitcast.107), channel_id=1, replica_groups=mesh['ctx'=16,'tp'=16] {'tp'}, dimensions={0} | all-to-all | bytes 1048576 | tf_op jit(solution)/shard_map/all_to_all | solution.py:131
  (116 shorter events, 14.4 us)
Async XLA Ops:
  6.5 142.9 %all-gather.3.cloned.1.call-start = ((), (), s32[]{:S(2)}) async-start(), calls=%async_computation.3 | async-start | bytes 4456448 | tf_op jit(solution)/shard_map/all_gather | solution.py:62
  8.8 8.4 %collective-permute-start = (bf16[512,64]{0,1:T(8,128)(2,1)S(1)}, bf16[512,64]{0,1:T(8,128)(2,1)S(1)}, u32[]{:S(2)}, u32[]{:S(2)}) collective-permute-start(bf16[512,64]{0,1:T(8,128)(2,1)S(1)} %constant_dynamic-update-slice_fusion), channel_id=1, source_target_pairs={{0,16},{16,32},{32,48},{48,64},{64,80},{80,96},{96,112},{112,128},... | collective-permute-start | bytes 196616 | tf_op jit(solution)/shard_map/ppermute | solution.py:56
  8.8 11.3 %collective-permute-start.1 = (bf16[512,64]{0,1:T(8,128)(2,1)S(1)}, bf16[512,64]{0,1:T(8,128)(2,1)S(1)}, u32[]{:S(2)}, u32[]{:S(2)}) collective-permute-start(bf16[512,64]{0,1:T(8,128)(2,1)S(1)} %constant_dynamic-update-slice_fusion), channel_id=1, source_target_pairs={{0,32},{16,48},{32,64},{48,80},{64,96},{80,112},{96,128},{112,144}... | collective-permute-start | bytes 196616 | tf_op jit(solution)/shard_map/ppermute | solution.py:56
  10.3 9.9 %collective-permute-start.2 = (bf16[512,64]{0,1:T(8,128)(2,1)S(1)}, bf16[512,64]{0,1:T(8,128)(2,1)S(1)}, u32[]{:S(2)}, u32[]{:S(2)}) collective-permute-start(bf16[512,64]{0,1:T(8,128)(2,1)S(1)} %constant_dynamic-update-slice_fusion), channel_id=1, source_target_pairs={{0,48},{16,64},{32,80},{48,96},{64,112},{80,128},{96,144},{112,160... | collective-permute-start | bytes 196616 | tf_op jit(solution)/shard_map/ppermute | solution.py:56
  12.4 9.3 %collective-permute-start.3 = (bf16[512,64]{0,1:T(8,128)(2,1)S(1)}, bf16[512,64]{0,1:T(8,128)(2,1)S(1)}, u32[]{:S(2)}, u32[]{:S(2)}) collective-permute-start(bf16[512,64]{0,1:T(8,128)(2,1)S(1)} %constant_dynamic-update-slice_fusion), channel_id=1, source_target_pairs={{0,64},{16,80},{32,96},{48,112},{64,128},{80,144},{96,160},{112,17... | collective-permute-start | bytes 196616 | tf_op jit(solution)/shard_map/ppermute | solution.py:56
  14.5 7.7 %collective-permute-start.4 = (bf16[512,64]{0,1:T(8,128)(2,1)S(1)}, bf16[512,64]{0,1:T(8,128)(2,1)S(1)}, u32[]{:S(2)}, u32[]{:S(2)}) collective-permute-start(bf16[512,64]{0,1:T(8,128)(2,1)S(1)} %constant_dynamic-update-slice_fusion), channel_id=1, source_target_pairs={{0,80},{16,96},{32,112},{48,128},{64,144},{80,160},{96,176},{112,1... | collective-permute-start | bytes 196616 | tf_op jit(solution)/shard_map/ppermute | solution.py:56
  17.2 6.8 %collective-permute-start.5 = (bf16[512,64]{0,1:T(8,128)(2,1)S(1)}, bf16[512,64]{0,1:T(8,128)(2,1)S(1)}, u32[]{:S(2)}, u32[]{:S(2)}) collective-permute-start(bf16[512,64]{0,1:T(8,128)(2,1)S(1)} %constant_dynamic-update-slice_fusion), channel_id=1, source_target_pairs={{0,96},{16,112},{32,128},{48,144},{64,160},{80,176},{96,192},{112,... | collective-permute-start | bytes 196616 | tf_op jit(solution)/shard_map/ppermute | solution.py:56
  20.1 5.7 %collective-permute-start.6 = (bf16[512,64]{0,1:T(8,128)(2,1)S(1)}, bf16[512,64]{0,1:T(8,128)(2,1)S(1)}, u32[]{:S(2)}, u32[]{:S(2)}) collective-permute-start(bf16[512,64]{0,1:T(8,128)(2,1)S(1)} %constant_dynamic-update-slice_fusion), channel_id=1, source_target_pairs={{0,112},{16,128},{32,144},{48,160},{64,176},{80,192},{96,208},{112... | collective-permute-start | bytes 196616 | tf_op jit(solution)/shard_map/ppermute | solution.py:56
  20.2 8.1 %collective-permute-start.7 = (bf16[512,64]{0,1:T(8,128)(2,1)S(1)}, bf16[512,64]{0,1:T(8,128)(2,1)S(1)}, u32[]{:S(2)}, u32[]{:S(2)}) collective-permute-start(bf16[512,64]{0,1:T(8,128)(2,1)S(1)} %constant_dynamic-update-slice_fusion), channel_id=1, source_target_pairs={{0,128},{16,144},{32,160},{48,176},{64,192},{80,208},{96,224},{112... | collective-permute-start | bytes 196616 | tf_op jit(solution)/shard_map/ppermute | solution.py:56
  21.7 7.9 %collective-permute-start.8 = (bf16[512,64]{0,1:T(8,128)(2,1)S(1)}, bf16[512,64]{0,1:T(8,128)(2,1)S(1)}, u32[]{:S(2)}, u32[]{:S(2)}) collective-permute-start(bf16[512,64]{0,1:T(8,128)(2,1)S(1)} %constant_dynamic-update-slice_fusion), channel_id=1, source_target_pairs={{0,144},{16,160},{32,176},{48,192},{64,208},{80,224},{96,240},{112... | collective-permute-start | bytes 196616 | tf_op jit(solution)/shard_map/ppermute | solution.py:56
  22.2 9.9 %collective-permute-start.9 = (bf16[512,64]{0,1:T(8,128)(2,1)S(1)}, bf16[512,64]{0,1:T(8,128)(2,1)S(1)}, u32[]{:S(2)}, u32[]{:S(2)}) collective-permute-start(bf16[512,64]{0,1:T(8,128)(2,1)S(1)} %constant_dynamic-update-slice_fusion), channel_id=1, source_target_pairs={{0,160},{16,176},{32,192},{48,208},{64,224},{80,240},{96,0},{112,1... | collective-permute-start | bytes 196616 | tf_op jit(solution)/shard_map/ppermute | solution.py:56
  24.0 9.3 %collective-permute-start.10 = (bf16[512,64]{0,1:T(8,128)(2,1)S(1)}, bf16[512,64]{0,1:T(8,128)(2,1)S(1)}, u32[]{:S(2)}, u32[]{:S(2)}) collective-permute-start(bf16[512,64]{0,1:T(8,128)(2,1)S(1)} %constant_dynamic-update-slice_fusion), channel_id=1, source_target_pairs={{0,176},{16,192},{32,208},{48,224},{64,240},{80,0},{96,16},{112,32... | collective-permute-start | bytes 196616 | tf_op jit(solution)/shard_map/ppermute | solution.py:56
  25.8 16.0 %collective-permute-start.11 = (bf16[512,64]{0,1:T(8,128)(2,1)S(1)}, bf16[512,64]{0,1:T(8,128)(2,1)S(1)}, u32[]{:S(2)}, u32[]{:S(2)}) collective-permute-start(bf16[512,64]{0,1:T(8,128)(2,1)S(1)} %constant_dynamic-update-slice_fusion), channel_id=1, source_target_pairs={{0,192},{16,208},{32,224},{48,240},{64,0},{80,16},{96,32},{112,48}... | collective-permute-start | bytes 196616 | tf_op jit(solution)/shard_map/ppermute | solution.py:56
  28.3 13.5 %collective-permute-start.12 = (bf16[512,64]{0,1:T(8,128)(2,1)S(1)}, bf16[512,64]{0,1:T(8,128)(2,1)S(1)}, u32[]{:S(2)}, u32[]{:S(2)}) collective-permute-start(bf16[512,64]{0,1:T(8,128)(2,1)S(1)} %constant_dynamic-update-slice_fusion), channel_id=1, source_target_pairs={{0,208},{16,224},{32,240},{48,0},{64,16},{80,32},{96,48},{112,64},... | collective-permute-start | bytes 196616 | tf_op jit(solution)/shard_map/ppermute | solution.py:56
  29.6 12.2 %collective-permute-start.13 = (bf16[512,64]{0,1:T(8,128)(2,1)S(1)}, bf16[512,64]{0,1:T(8,128)(2,1)S(1)}, u32[]{:S(2)}, u32[]{:S(2)}) collective-permute-start(bf16[512,64]{0,1:T(8,128)(2,1)S(1)} %constant_dynamic-update-slice_fusion), channel_id=1, source_target_pairs={{0,224},{16,240},{32,0},{48,16},{64,32},{80,48},{96,64},{112,80},{... | collective-permute-start | bytes 196616 | tf_op jit(solution)/shard_map/ppermute | solution.py:56
  32.0 11.9 %collective-permute-start.14 = (bf16[512,64]{0,1:T(8,128)(2,1)S(1)}, bf16[512,64]{0,1:T(8,128)(2,1)S(1)}, u32[]{:S(2)}, u32[]{:S(2)}) collective-permute-start(bf16[512,64]{0,1:T(8,128)(2,1)S(1)} %constant_dynamic-update-slice_fusion), channel_id=1, source_target_pairs={{0,240},{16,0},{32,16},{48,32},{64,48},{80,64},{96,80},{112,96},{1... | collective-permute-start | bytes 196616 | tf_op jit(solution)/shard_map/ppermute | solution.py:56
  33.3 53.3 %collective-permute-start.23 = (bf16[256,512]{1,0:T(8,128)(2,1)}, bf16[256,512]{1,0:T(8,128)(2,1)S(1)}, u32[]{:S(2)}, u32[]{:S(2)}) collective-permute-start(bf16[256,512]{1,0:T(8,128)(2,1)} %param.13), channel_id=1, source_target_pairs={{0,0},{1,16},{2,32},{3,48},{4,64},{5,80},{6,96},{7,112},{8,128},{9... | collective-permute-start | bytes 786440 | tf_op jit(solution)/shard_map/ppermute | solution.py:118
  52.2 26.2 %all-to-all-start = ((bf16[16,512,2,8]{1,3,2,0:T(8,128)(2,1)}), bf16[16,512,2,8]{1,3,2,0:T(8,128)(2,1)S(1)}, u32[]{:S(2)}, u32[]{:S(2)}) async-start(bf16[16,512,2,8]{1,3,2,0:T(8,128)(2,1)} %broadcast_select_fusion), calls=%async_computation | async-start | bytes 524288 | tf_op jit(solution)/shard_map/all_to_all | solution.py:72
  66.6 114.7 %all-gather.5.cloned.1.call-start = ((), (), s32[]{:S(2)}) async-start(), calls=%async_computation.4 | async-start | bytes 4456448 | tf_op jit(solution)/shard_map/all_gather | solution.py:123
  79.1 12.1 %collective-permute-start.15 = (bf16[512,256]{0,1:T(8,128)(2,1)S(1)}, bf16[512,256]{0,1:T(8,128)(2,1)S(1)}, u32[]{:S(2)}, u32[]{:S(2)}) collective-permute-start(bf16[512,256]{0,1:T(8,128)(2,1)S(1)} %pad_maximum_fusion), channel_id=1, source_target_pairs={{0,128},{16,144},{32,160},{48,176},{64,192},{80,208},{96,224},{112... | collective-permute-start | bytes 786440 | tf_op jit(solution)/shard_map/ppermute | solution.py:85
  81.0 12.2 %collective-permute-start.16 = (bf16[512,256]{0,1:T(8,128)(2,1)S(1)}, bf16[512,256]{0,1:T(8,128)(2,1)S(1)}, u32[]{:S(2)}, u32[]{:S(2)}) collective-permute-start(bf16[512,256]{0,1:T(8,128)(2,1)S(1)} %pad_maximum_fusion), channel_id=1, source_target_pairs={{0,112},{16,128},{32,144},{48,160},{64,176},{80,192},{96,208},{112... | collective-permute-start | bytes 786440 | tf_op jit(solution)/shard_map/ppermute | solution.py:85
  84.6 12.7 %collective-permute-start.17 = (bf16[512,256]{0,1:T(8,128)(2,1)S(1)}, bf16[512,256]{0,1:T(8,128)(2,1)S(1)}, u32[]{:S(2)}, u32[]{:S(2)}) collective-permute-start(bf16[512,256]{0,1:T(8,128)(2,1)S(1)} %pad_maximum_fusion), channel_id=1, source_target_pairs={{0,96},{16,112},{32,128},{48,144},{64,160},{80,176},{96,192},{112,... | collective-permute-start | bytes 786440 | tf_op jit(solution)/shard_map/ppermute | solution.py:85
  86.6 0.7 copy-start.3
  87.3 11.9 %collective-permute-start.18 = (bf16[512,256]{0,1:T(8,128)(2,1)S(1)}, bf16[512,256]{0,1:T(8,128)(2,1)S(1)}, u32[]{:S(2)}, u32[]{:S(2)}) collective-permute-start(bf16[512,256]{0,1:T(8,128)(2,1)S(1)} %pad_maximum_fusion), channel_id=1, source_target_pairs={{0,80},{16,96},{32,112},{48,128},{64,144},{80,160},{96,176},{112,1... | collective-permute-start | bytes 786440 | tf_op jit(solution)/shard_map/ppermute | solution.py:85
  89.2 17.6 %collective-permute-start.19 = (bf16[512,256]{0,1:T(8,128)(2,1)S(1)}, bf16[512,256]{0,1:T(8,128)(2,1)S(1)}, u32[]{:S(2)}, u32[]{:S(2)}) collective-permute-start(bf16[512,256]{0,1:T(8,128)(2,1)S(1)} %pad_maximum_fusion), channel_id=1, source_target_pairs={{0,64},{16,80},{32,96},{48,112},{64,128},{80,144},{96,160},{112,17... | collective-permute-start | bytes 786440 | tf_op jit(solution)/shard_map/ppermute | solution.py:85
  91.2 26.9 %collective-permute-start.20 = (bf16[512,256]{0,1:T(8,128)(2,1)S(1)}, bf16[512,256]{0,1:T(8,128)(2,1)S(1)}, u32[]{:S(2)}, u32[]{:S(2)}) collective-permute-start(bf16[512,256]{0,1:T(8,128)(2,1)S(1)} %pad_maximum_fusion), channel_id=1, source_target_pairs={{0,48},{16,64},{32,80},{48,96},{64,112},{80,128},{96,144},{112,160... | collective-permute-start | bytes 786440 | tf_op jit(solution)/shard_map/ppermute | solution.py:85
  93.2 52.3 %collective-permute-start.21 = (bf16[512,256]{0,1:T(8,128)(2,1)S(1)}, bf16[512,256]{0,1:T(8,128)(2,1)S(1)}, u32[]{:S(2)}, u32[]{:S(2)}) collective-permute-start(bf16[512,256]{0,1:T(8,128)(2,1)S(1)} %pad_maximum_fusion), channel_id=1, source_target_pairs={{0,32},{16,48},{32,64},{48,80},{64,96},{80,112},{96,128},{112,144}... | collective-permute-start | bytes 786440 | tf_op jit(solution)/shard_map/ppermute | solution.py:85
  97.3 50.4 %collective-permute-start.22 = (bf16[512,256]{0,1:T(8,128)(2,1)S(1)}, bf16[512,256]{0,1:T(8,128)(2,1)S(1)}, u32[]{:S(2)}, u32[]{:S(2)}) collective-permute-start(bf16[512,256]{0,1:T(8,128)(2,1)S(1)} %pad_maximum_fusion), channel_id=1, source_target_pairs={{0,16},{16,32},{32,48},{48,64},{64,80},{80,96},{96,112},{112,128},... | collective-permute-start | bytes 786440 | tf_op jit(solution)/shard_map/ppermute | solution.py:85
  149.4 7.1 %copy-start.1 = (f32[512,64]{0,1:T(8,128)S(1)}, f32[512,64]{0,1:T(8,128)}, u32[]{:S(2)}) copy-start(f32[512,64]{0,1:T(8,128)} %get-tuple-element.131) | copy-start | bytes 393220
  149.4 7.1 %copy-start.2 = (f32[512,64]{0,1:T(8,128)S(1)}, f32[512,64]{0,1:T(8,128)}, u32[]{:S(2)}) copy-start(f32[512,64]{0,1:T(8,128)} %get-tuple-element.132) | copy-start | bytes 393220
  149.4 7.4 %copy-start = (s32[4608]{0:T(1024)S(1)}, s32[4608]{0:T(1024)}, u32[]{:S(2)}) copy-start(s32[4608]{0:T(1024)} %compare_select_fusion) | copy-start | bytes 55300
  149.4 7.4 %copy-start.4 = (bf16[4,256,128]{2,1,0:T(8,128)(2,1)S(1)}, bf16[4,256,128]{2,1,0:T(8,128)(2,1)}, u32[]{:S(2)}) copy-start(bf16[4,256,128]{2,1,0:T(8,128)(2,1)} %custom-call.7) | copy-start | bytes 786436
  176.7 91.3 %all-to-all-start.1 = ((bf16[16,512,256]{1,2,0:T(8,128)(2,1)}), bf16[16,512,256]{1,2,0:T(8,128)(2,1)}, u32[]{:S(2)}, u32[]{:S(2)}) async-start(bf16[16,512,256]{1,2,0:T(8,128)(2,1)} %stack.71), calls=%async_computation.1 | async-start | bytes 8388608 | tf_op jit(solution)/shard_map/all_to_all | solution.py:15
Sparse Core Ops, SparseCore 0:
  9.2 54.0 all-gather.2
  87.4 52.9 all-gather.4
